TPU v7x, 512 devices: a whole 4x4x16 slice. The times are simulated.
512 devices in a mesh: exp: 16 (over z), sky: 32 (over y, x, core).
Axes of the slice: x: 4, y: 4, z: 16, core: 2. Of those that a mesh axis runs over, the one named last changes fastest.
Arguments:
- sky_start: float32 [16, 128, 4096], P(None, None, 'sky'), may hold values from -6 to 6
- exposures: bfloat16 [16, 1024, 2, 128, 128], P('exp', 'sky'), may hold values from -16 to 16
- weights: bfloat16 [16, 1024, 2], P('exp', 'sky'), may hold values from 0.5 to 2
- footprint_owner: int32 [16, 1024, 1], P('exp', 'sky'), may hold values from 0 to 31; in each aligned block of 32 rows (0 to 31, 32 to 63, ..., all dimensions but the last counted through in order) at most 2 rows name the same one
- footprint_row: int32 [16, 1024], P('exp', 'sky'), may hold values from 0 to 15
- kernel_index: int32 [16, 1024, 2, 2], P('exp', 'sky'), may hold values from 0 to 7
- kernels: bfloat16 [8, 128, 128], replicated, may hold values from -1 to 1
Outputs:
- sky_image: float32 [16, 128, 4096], P(None, None, 'sky')
Inputs may be any that keep to these rules, and one draw needn't show every extreme that they name: `footprint_owner`: the 32 footprint tiles of one device name one tile column at most 2 times, and some tile column exactly 2 times.
All inputs are finite; a program needn't handle non-finite values.
Results may differ from a plain program's by a relative error of at most 0.0035.
Values may be sent and summed in bfloat16 or wider, within the bound.
No kernel may reach another device: no remote copies, remote signals or barrier semaphores. Data moves between devices by JAX's collectives and lax.ppermute only.
A program may use at most 128 MiB of HBM per device.

v0:
```python
import jax
import jax.numpy as jnp
from jax import lax
from jax.sharding import PartitionSpec as P

ITERS = 2
weight_ceiling = 2.0


def padded_2(cells, sides, width):
    for axis, dim in sides:
        count = lax.axis_size(axis)
        ends = count - 1
        head = lax.slice_in_dim(cells, 0, width, axis=dim)
        tail = lax.slice_in_dim(cells, cells.shape[dim] - width, cells.shape[dim], axis=dim)
        cells = jnp.concatenate(
            [
                lax.ppermute(tail, axis, [(i, (i + 1) % count) for i in range(ends)]),
                cells,
                lax.ppermute(head, axis, [((i + 1) % count, i) for i in range(ends)]),
            ],
            axis=dim,
        )
    return cells


def pick_kernels(kernel_ids, kernels):
    table_size = kernels.shape[0]
    tile_edge = kernels.shape[1]
    onehot = (kernel_ids[..., None] == jnp.arange(table_size, dtype=jnp.int32)).astype(jnp.bfloat16)
    onehot = onehot.reshape(-1, table_size)
    selected = jnp.dot(onehot, kernels.reshape(table_size, -1), preferred_element_type=jnp.float32)
    selected = selected.astype(jnp.bfloat16).reshape(kernel_ids.shape + (tile_edge, tile_edge))
    return (selected[..., 0, :, :], selected[..., 1, :, :])


def adjoint_tiles(fetched, left_kernels, right_kernels, tile_weights, observed):
    left_product = jnp.einsum(
        "fetu,fuv->fetv", left_kernels, fetched, preferred_element_type=jnp.float32
    ).astype(jnp.bfloat16)
    predicted = jnp.einsum(
        "fetv,fewv->fetw", left_product, right_kernels, preferred_element_type=jnp.float32
    )
    residual = tile_weights.astype(jnp.float32)[..., None, None] * (
        predicted - observed.astype(jnp.float32)
    )
    residual = residual.astype(jnp.bfloat16)
    back_product = jnp.einsum(
        "feut,feuw->fetw", left_kernels, residual, preferred_element_type=jnp.float32
    ).astype(jnp.bfloat16)
    summed = jnp.sum(
        jnp.einsum(
            "fetw,fewv->fetv", back_product, right_kernels, preferred_element_type=jnp.float32
        ),
        axis=1,
    )
    return summed.astype(jnp.bfloat16)


def laplace_image(padded):
    image_rows = padded.reshape(padded.shape[0] * padded.shape[1], padded.shape[2])
    center = image_rows[:, 1:-1]
    vertical = jnp.pad(center, ((1, 1), (0, 0)))
    laplacian = 4.0 * center - image_rows[:, :-2] - image_rows[:, 2:] - vertical[:-2] - vertical[2:]
    return laplacian.reshape(padded.shape[0], padded.shape[1], padded.shape[2] - 2)


def per_device(
    sky_start, exposures, weights, footprint_owner, footprint_row, kernel_index, kernels
):
    sky_rows = sky_start.shape[0]
    tile_edge = sky_start.shape[1]
    foot_tiles = footprint_row.shape[1]
    expo_count = exposures.shape[2]
    n_sky = lax.axis_size("sky")
    n_exp = lax.axis_size("exp")
    capacity = max(2, 3 * foot_tiles // (2 * n_sky))
    slot_count = n_sky * capacity
    prior_weight = n_exp * foot_tiles * expo_count / (8.0 * sky_rows)
    owner_ids = footprint_owner[0, :, 0]
    tile_rows = footprint_row[0]
    onehot_owner = (owner_ids[:, None] == jnp.arange(n_sky, dtype=jnp.int32)[None, :]).astype(
        jnp.int32
    )
    ranks = jnp.sum((jnp.cumsum(onehot_owner, axis=0) - onehot_owner) * onehot_owner, axis=1)
    slot_of = owner_ids * capacity + ranks
    packing = jnp.arange(slot_count, dtype=jnp.int32)[:, None] == slot_of[None, :]
    requested = jnp.sum(jnp.where(packing, tile_rows[None, :] + 1, 0), axis=1) - 1
    slot_source = jnp.sum(jnp.where(packing, jnp.arange(foot_tiles)[None, :] + 1, 0), axis=1) - 1
    slot_source = jnp.where(slot_source < 0, foot_tiles, slot_source)
    observed = exposures[0]
    tile_weights = weights[0]
    kernel_ids = kernel_index[0]
    incoming = lax.all_to_all(requested, "sky", split_axis=0, concat_axis=0, tiled=True)
    left_kernels, right_kernels = pick_kernels(kernel_ids, kernels)
    receive_map = jnp.arange(sky_rows, dtype=jnp.int32)[:, None] == incoming[None, :]
    local_counts = float(expo_count) * jnp.sum(receive_map.astype(jnp.float32), axis=1)
    receive_half = receive_map.astype(jnp.bfloat16)
    safe_rows = jnp.maximum(incoming, 0)
    rows_per = sky_rows // n_exp
    own_rows = lax.axis_index("exp") * rows_per
    count_tile = jnp.broadcast_to(local_counts[:, None], (sky_rows, tile_edge))
    sky_now = sky_start
    for iteration in range(ITERS):
        replies = lax.all_to_all(
            sky_now[safe_rows].astype(jnp.bfloat16), "sky", split_axis=0, concat_axis=0, tiled=True
        )
        fetched = replies[slot_of]
        adjoint = adjoint_tiles(fetched, left_kernels, right_kernels, tile_weights, observed)
        outgoing = jnp.where(
            (slot_source < foot_tiles)[:, None, None],
            adjoint[jnp.minimum(slot_source, foot_tiles - 1)],
            jnp.zeros((), adjoint.dtype),
        )
        arrived = lax.all_to_all(outgoing, "sky", split_axis=0, concat_axis=0, tiled=True)
        if iteration == 0:
            count_tiles = lax.all_gather(count_tile, "exp", axis=0, tiled=True)
            count_tiles, arrived = lax.optimization_barrier((count_tiles, arrived))
            counts = jnp.sum(
                count_tiles.astype(jnp.float32).reshape(n_exp, sky_rows, tile_edge)[:, :, 0], axis=0
            )
            denominator = weight_ceiling * counts + 8.0 * prior_weight
            own_denominator = lax.dynamic_slice_in_dim(denominator, own_rows, rows_per)
        partial_value = jnp.einsum(
            "rj,juv->ruv", receive_half, arrived, preferred_element_type=jnp.float32
        )
        payload = partial_value.astype(jnp.bfloat16).reshape(n_exp, rows_per * tile_edge, tile_edge)
        row_parts = lax.all_to_all(payload, "exp", split_axis=0, concat_axis=0, tiled=True)
        summed = jnp.sum(
            row_parts.astype(jnp.float32).reshape((n_exp,) + payload.shape[1:]), axis=0
        )
        own_total = summed[: rows_per * tile_edge].reshape(rows_per, tile_edge, tile_edge)
        scaled = own_total / own_denominator[:, None, None]
        gathered = lax.all_gather(scaled.astype(jnp.bfloat16), "exp", axis=0, tiled=True)
        laplacian = laplace_image(padded_2(sky_now, (("sky", 2),), 1))
        smooth = prior_weight * laplacian / denominator[:, None, None]
        sky_now = sky_now - (gathered.astype(jnp.float32) + smooth)
    return sky_now


def solution(mesh):
    in_specs = (
        P(None, None, "sky"),
        P("exp", "sky", None, None, None),
        P("exp", "sky", None),
        P("exp", "sky", None),
        P("exp", "sky"),
        P("exp", "sky", None, None),
        P(),
    )
    out_specs = P(None, None, "sky")
    return jax.shard_map(
        per_device, mesh=mesh, in_specs=in_specs, out_specs=out_specs, check_vma=False
    )
```

profile of v0, /device:TPU:2, one launch (start us, length us, event | category | flops | bytes accessed | tf_op | source)
XLA Modules:
  0.0 339.1 jit_solution(3702893933402710310)
XLA Ops:
  0.0 0.7 fusion.48
  0.8 0.8 select_reduce_fusion.2
  1.6 0.7 iota_add_fusion
  2.3 0.7 add_bitcast_fusion
  3.1 14.8 %all_to_all.36 = s32[32,2,1]{1,2,0:T(1,128)S(1)} all-to-all(s32[32,2,1]{1,2,0:T(1,128)S(1)} %bitcast.102), channel_id=1, replica_groups=mesh['exp'=16,'sky'=32] {'sky'}, dimensions={0} | all-to-all | bytes 512 | tf_op jit(solution)/shard_map/all_to_all | solution.py:94
  18.4 0.7 maximum_reduce_fusion
  19.3 3.3 gather_fusion
  22.6 5.2 %all-to-all-start.1 = ((bf16[64,128,128]{2,1,0:T(8,128)(2,1)}), bf16[64,128,128]{2,1,0:T(8,128)(2,1)S(1)}, u32[]{:S(2)}, u32[]{:S(2)}) async-start(bf16[64,128,128]{2,1,0:T(8,128)(2,1)} %gather_fusion), calls=%async_computation.1 | async-start | bytes 4194304 | tf_op jit(solution)/shard_map/all_to_all | solution.py:105
  28.2 1.3 fusion.4
  29.6 3.2 copy.109
  32.8 23.1 %all-to-all-done.1 = bf16[64,128,128]{2,1,0:T(8,128)(2,1)S(1)} async-done(((bf16[64,128,128]{2,1,0:T(8,128)(2,1)}), bf16[64,128,128]{2,1,0:T(8,128)(2,1)S(1)}, u32[]{:S(2)}, u32[]{:S(2)}) %all-to-all-start.1) | async-done | bytes 2097184 | tf_op jit(solution)/shard_map/all_to_all | solution.py:105
  55.8 0.7 gather_fusion.1
  56.6 5.0 %fusion.1 = bf16[32,2,128,128]{3,2,1,0:T(8,128)(2,1)S(1)} fusion(bf16[1,32,2,128,128]{4,3,2,1,0:T(8,128)(2,1)} %param.8, f32[32,2]{1,0:T(8,128)S(1)} %copy.80, bf16[32,2,2,128,128]{4,3,2,1,0:T(8,128)(2,1)} %bitcast.92, bf16[32,128,128]{2,1,0:T(8,128)(2,1)S(1)} %gather_fusion.1), kind=kOutput, calls=%fused_computation.10 | convolution fusion | flops 542113792 | bytes 9437440 | tf_op jit(solution)/shard_map/fetv,fewv->fetw/dot_general | solution.py:41
  61.6 3.6 %bitcast_convert_fusion.1 = bf16[32,128,128]{2,1,0:T(8,128)(2,1)S(1)} fusion(bf16[32,2,128,128]{3,2,1,0:T(8,128)(2,1)S(1)} %fusion.1, bf16[32,2,2,128,128]{4,3,2,1,0:T(8,128)(2,1)} %bitcast.93), kind=kOutput, calls=%fused_computation.19 | convolution fusion | flops 538443776 | bytes 7340032 | tf_op jit(solution)/shard_map/fetw,fewv->fetv/dot_general | solution.py:52
  65.3 1.0 gather_fusion.2
  66.2 1.5 broadcast_select_fusion.1
  67.8 6.0 %all-to-all-start.2 = ((bf16[64,128,128]{2,1,0:T(8,128)(2,1)}), bf16[64,128,128]{2,1,0:T(8,128)(2,1)S(1)}, u32[]{:S(2)}, u32[]{:S(2)}) async-start(bf16[64,128,128]{2,1,0:T(8,128)(2,1)} %broadcast_select_fusion.1), calls=%async_computation.2 | async-start | bytes 4194304 | tf_op jit(solution)/shard_map/all_to_all | solution.py:115
  73.8 1.3 dynamic-slice
  76.1 35.3 %all-reduce.2 = f32[256]{0:T(256)S(1)} all-reduce(f32[256]{0:T(256)S(1)} %multiply_dynamic-update-slice_fusion), channel_id=2, replica_groups=mesh['exp'=16,'sky'=32] {'exp'}, use_global_device_ids=true, to_apply=%add.2 | all-reduce | flops 256 | bytes 2048
  111.4 1.3 fusion.27
  112.7 0.9 copy.84
  113.6 6.8 %all-to-all-start.3 = ((bf16[16,128,128]{2,1,0:T(8,128)(2,1)}), bf16[16,128,128]{2,1,0:T(8,128)(2,1)}, u32[]{:S(2)}, u32[]{:S(2)}) async-start(bf16[16,128,128]{2,1,0:T(8,128)(2,1)} %copy.84), calls=%async_computation.3 | async-start | bytes 1048576 | tf_op jit(solution)/shard_map/all_to_all | solution.py:128
  121.1 1.9 collective-permute-start.1
  123.4 2.6 collective-permute-start
  126.3 2.0 collective-permute-done
  128.7 0.9 pad_maximum_fusion
  131.1 15.0 %all-to-all-done.3 = bf16[16,128,128]{2,1,0:T(8,128)(2,1)} async-done(((bf16[16,128,128]{2,1,0:T(8,128)(2,1)}), bf16[16,128,128]{2,1,0:T(8,128)(2,1)}, u32[]{:S(2)}, u32[]{:S(2)}) %all-to-all-start.3) | async-done | bytes 524320 | tf_op jit(solution)/shard_map/all_to_all | solution.py:128
  146.1 1.1 convert_reduce_fusion.1
  147.8 32.3 %all-gather = bf16[2048,128]{1,0:T(8,128)(2,1)S(1)} all-gather(bf16[128,128]{1,0:T(8,128)(2,1)S(1)} %divide_convert_fusion.1), channel_id=3, replica_groups=mesh['exp'=16,'sky'=32] {'exp'}, dimensions={0}, use_global_device_ids=true | all-gather | bytes 557056 | tf_op jit(solution)/shard_map/all_gather | solution.py:134
  180.4 2.1 gather_fusion.3
  182.5 33.0 %all_to_all.37 = bf16[64,128,128]{2,1,0:T(8,128)(2,1)} all-to-all(bf16[64,128,128]{2,1,0:T(8,128)(2,1)} %gather_fusion.3), channel_id=1, replica_groups=mesh['exp'=16,'sky'=32] {'sky'}, dimensions={0} | all-to-all | bytes 4194304 | tf_op jit(solution)/shard_map/all_to_all | solution.py:105
  215.5 2.3 gather_fusion.4
  217.8 6.3 %fusion.3 = bf16[32,2,128,128]{3,2,1,0:T(8,128)(2,1)} fusion(bf16[1,32,2,128,128]{4,3,2,1,0:T(8,128)(2,1)} %param.8, f32[32,2]{1,0:T(8,128)S(1)} %copy.80, bf16[32,2,2,128,128]{4,3,2,1,0:T(8,128)(2,1)} %bitcast.94, bf16[32,128,128]{2,1,0:T(8,128)(2,1)S(1)} %gather_fusion.4), kind=kOutput, calls=%fused_computation.12 | convolution fusion | flops 542113792 | bytes 9437440 | tf_op jit(solution)/shard_map/fetv,fewv->fetw/dot_general | solution.py:41
  224.2 4.3 %bitcast_convert_fusion = bf16[32,128,128]{2,1,0:T(8,128)(2,1)S(1)} fusion(bf16[32,2,128,128]{3,2,1,0:T(8,128)(2,1)} %fusion.3, bf16[32,2,2,128,128]{4,3,2,1,0:T(8,128)(2,1)} %bitcast.95), kind=kOutput, calls=%fused_computation.18 | convolution fusion | flops 538443776 | bytes 7340032 | tf_op jit(solution)/shard_map/fetw,fewv->fetv/dot_general | solution.py:52
  228.4 2.2 gather_fusion.5
  230.6 1.8 broadcast_select_fusion
  232.4 31.9 %all_to_all.38 = bf16[64,128,128]{2,1,0:T(8,128)(2,1)S(1)} all-to-all(bf16[64,128,128]{2,1,0:T(8,128)(2,1)S(1)} %broadcast_select_fusion), channel_id=1, replica_groups=mesh['exp'=16,'sky'=32] {'sky'}, dimensions={0} | all-to-all | bytes 4194304 | tf_op jit(solution)/shard_map/all_to_all | solution.py:115
  264.4 1.3 fusion.30
  265.6 0.9 copy.92
  266.5 6.7 %all-to-all-start.6 = ((bf16[16,128,128]{2,1,0:T(8,128)(2,1)}), bf16[16,128,128]{2,1,0:T(8,128)(2,1)}, u32[]{:S(2)}, u32[]{:S(2)}) async-start(bf16[16,128,128]{2,1,0:T(8,128)(2,1)} %copy.92), calls=%async_computation.6 | async-start | bytes 1048576 | tf_op jit(solution)/shard_map/all_to_all | solution.py:128
  273.9 2.8 collective-permute-start.3
  277.1 2.1 collective-permute-start.2
  279.6 2.4 collective-permute-done.2
  282.4 0.9 pad_maximum_fusion.1
  284.1 18.4 %all-to-all-done.6 = bf16[16,128,128]{2,1,0:T(8,128)(2,1)} async-done(((bf16[16,128,128]{2,1,0:T(8,128)(2,1)}), bf16[16,128,128]{2,1,0:T(8,128)(2,1)}, u32[]{:S(2)}, u32[]{:S(2)}) %all-to-all-start.6) | async-done | bytes 524320 | tf_op jit(solution)/shard_map/all_to_all | solution.py:128
  302.5 1.1 convert_reduce_fusion
  304.2 33.6 %all-gather.1 = bf16[2048,128]{1,0:T(8,128)(2,1)S(1)} all-gather(bf16[128,128]{1,0:T(8,128)(2,1)S(1)} %divide_convert_fusion), channel_id=4, replica_groups=mesh['exp'=16,'sky'=32] {'exp'}, dimensions={0}, use_global_device_ids=true | all-gather | bytes 557056 | tf_op jit(solution)/shard_map/all_gather | solution.py:134
  337.9 1.2 fusion.39
  (54 shorter events, 8.9 us)
Async XLA Ops:
  22.6 5.3 %copy-start.4 = (bf16[1,32,2]{1,2,0:T(2,128)(2,1)S(1)}, bf16[1,32,2]{1,2,0:T(2,128)(2,1)}, u32[]{:S(2)}) copy-start(bf16[1,32,2]{1,2,0:T(2,128)(2,1)} %param.9) | copy-start | bytes 388
  22.6 5.4 %copy-start.3 = (s32[1,32,2,2]{1,3,2,0:T(2,128)S(1)}, s32[1,32,2,2]{1,3,2,0:T(2,128)}, u32[]{:S(2)}) copy-start(s32[1,32,2,2]{1,3,2,0:T(2,128)} %param.12) | copy-start | bytes 1540
  22.6 5.6 %copy-start.1 = (bf16[8,128,128]{2,1,0:T(8,128)(2,1)S(1)}, bf16[8,128,128]{2,1,0:T(8,128)(2,1)}, u32[]{:S(2)}) copy-start(bf16[8,128,128]{2,1,0:T(8,128)(2,1)} %param.13) | copy-start | bytes 786436
  22.6 33.2 %all-to-all-start.1 = ((bf16[64,128,128]{2,1,0:T(8,128)(2,1)}), bf16[64,128,128]{2,1,0:T(8,128)(2,1)S(1)}, u32[]{:S(2)}, u32[]{:S(2)}) async-start(bf16[64,128,128]{2,1,0:T(8,128)(2,1)} %gather_fusion), calls=%async_computation.1 | async-start | bytes 4194304 | tf_op jit(solution)/shard_map/all_to_all | solution.py:105
  29.5 3.2 copy-start.2
  67.8 43.6 %all-to-all-start.2 = ((bf16[64,128,128]{2,1,0:T(8,128)(2,1)}), bf16[64,128,128]{2,1,0:T(8,128)(2,1)S(1)}, u32[]{:S(2)}, u32[]{:S(2)}) async-start(bf16[64,128,128]{2,1,0:T(8,128)(2,1)} %broadcast_select_fusion.1), calls=%async_computation.2 | async-start | bytes 4194304 | tf_op jit(solution)/shard_map/all_to_all | solution.py:115
  111.4 9.0 %copy-start = (f32[16,128,128]{2,1,0:T(8,128)S(1)}, f32[16,128,128]{2,1,0:T(8,128)}, u32[]{:S(2)}) copy-start(f32[16,128,128]{2,1,0:T(8,128)} %param.7) | copy-start | bytes 3145732
  113.6 32.5 %all-to-all-start.3 = ((bf16[16,128,128]{2,1,0:T(8,128)(2,1)}), bf16[16,128,128]{2,1,0:T(8,128)(2,1)}, u32[]{:S(2)}, u32[]{:S(2)}) async-start(bf16[16,128,128]{2,1,0:T(8,128)(2,1)} %copy.84), calls=%async_computation.3 | async-start | bytes 1048576 | tf_op jit(solution)/shard_map/all_to_all | solution.py:128
  121.1 4.9 %collective-permute-start.1 = (f32[16,128,1]{1,0,2:T(8,128)S(1)}, f32[16,128,1]{1,0,2:T(8,128)S(1)}, u32[]{:S(2)}, u32[]{:S(2)}) collective-permute-start(f32[16,128,1]{1,0,2:T(8,128)S(1)} %copy.107), channel_id=1, source_target_pairs={{1,0},{2,1},{3,2},{4,3},{5,4},{6,5},{7,6},{8,7},{9,8},{10,9},{11,1... | collective-permute-start | bytes 24584 | tf_op jit(solution)/shard_map/ppermute | solution.py:20
  123.4 5.0 %collective-permute-start = (f32[16,128,1]{1,0,2:T(8,128)S(1)}, f32[16,128,1]{1,0,2:T(8,128)S(1)}, u32[]{:S(2)}, u32[]{:S(2)}) collective-permute-start(f32[16,128,1]{1,0,2:T(8,128)S(1)} %copy.106), channel_id=1, source_target_pairs={{0,1},{1,2},{2,3},{3,4},{4,5},{5,6},{6,7},{7,8},{8,9},{9,10},{10,1... | collective-permute-start | bytes 24584 | tf_op jit(solution)/shard_map/ppermute | solution.py:18
  266.5 36.0 %all-to-all-start.6 = ((bf16[16,128,128]{2,1,0:T(8,128)(2,1)}), bf16[16,128,128]{2,1,0:T(8,128)(2,1)}, u32[]{:S(2)}, u32[]{:S(2)}) async-start(bf16[16,128,128]{2,1,0:T(8,128)(2,1)} %copy.92), calls=%async_computation.6 | async-start | bytes 1048576 | tf_op jit(solution)/shard_map/all_to_all | solution.py:128
  273.9 5.3 %collective-permute-start.3 = (f32[16,128,1]{1,0,2:T(8,128)S(1)}, f32[16,128,1]{1,0,2:T(8,128)S(1)}, u32[]{:S(2)}, u32[]{:S(2)}) collective-permute-start(f32[16,128,1]{1,0,2:T(8,128)S(1)} %copy.94), channel_id=1, source_target_pairs={{1,0},{2,1},{3,2},{4,3},{5,4},{6,5},{7,6},{8,7},{9,8},{10,9},{11,1... | collective-permute-start | bytes 24584 | tf_op jit(solution)/shard_map/ppermute | solution.py:20
  277.1 5.0 %collective-permute-start.2 = (f32[16,128,1]{1,0,2:T(8,128)S(1)}, f32[16,128,1]{1,0,2:T(8,128)S(1)}, u32[]{:S(2)}, u32[]{:S(2)}) collective-permute-start(f32[16,128,1]{1,0,2:T(8,128)S(1)} %copy.93), channel_id=1, source_target_pairs={{0,1},{1,2},{2,3},{3,4},{4,5},{5,6},{6,7},{7,8},{8,9},{9,10},{10,1... | collective-permute-start | bytes 24584 | tf_op jit(solution)/shard_map/ppermute | solution.py:18
where the time goes:
time: 340 us; the launch traced here: 339 us
  blocking collectives  181 us (53%)
  waiting for transfers between devices  60.9 us (18%)
  starting transfers between devices  34.2 us (10%)
  local copies, waits for them, and re-layouts  23.9 us (7%)
  matrix products  23.1 us (7%)
  other arithmetic  15.1 us (4%)
    all_gather x2, blocking collectives, per_device(): lax.all_gather(scaled.astype(jnp.bfloat16), 'exp', axis=0, tiled=True)  65.9 us
    unnamed x1, blocking collectives  35.3 us
    all_to_all x2, waiting for transfers between devices, per_device(): lax.all_to_all(payload, 'exp', split_axis=0, concat_axis=0, tiled=True)  33.4 us
    all_to_all x1, blocking collectives, per_device(): lax.all_to_all(sky_now[safe_rows].astype(jnp.bfloat16), 'sky', split_axis...  33 us
    all_to_all x1, blocking collectives, per_device(): lax.all_to_all(outgoing, 'sky', split_axis=0, concat_axis=0, tiled=True)  31.9 us
    all_to_all x1, waiting for transfers between devices, per_device(): lax.all_to_all(sky_now[safe_rows].astype(jnp.bfloat16), 'sky', split_axis...  23.1 us
    all_to_all x1, blocking collectives, per_device(): lax.all_to_all(requested, 'sky', split_axis=0, concat_axis=0, tiled=True)  14.8 us
    all_to_all x2, starting transfers between devices, per_device(): lax.all_to_all(payload, 'exp', split_axis=0, concat_axis=0, tiled=True)  13.5 us
  transfers between devices with their start and end apart: 8, of which 5 were waited for; matrix products, arithmetic and copies ran while one was open for 4% of the time, Pallas kernels for 0%

commit v1 on v0

--- a/solution.py
+++ b/solution.py
@@ -5,6 +5,12 @@
 
 ITERS = 2
 weight_ceiling = 2.0
+
+
+def joined_along(blocks, dim):
+    lengths = list(blocks.shape[1:])
+    lengths[dim] *= blocks.shape[0]
+    return jnp.moveaxis(blocks, 0, dim).reshape(lengths)
 
 
 def padded_2(cells, sides, width):
@@ -131,7 +137,20 @@
         )
         own_total = summed[: rows_per * tile_edge].reshape(rows_per, tile_edge, tile_edge)
         scaled = own_total / own_denominator[:, None, None]
-        gathered = lax.all_gather(scaled.astype(jnp.bfloat16), "exp", axis=0, tiled=True)
+        shard = scaled.astype(jnp.bfloat16)
+        count_2 = lax.axis_size("exp")
+        pairs = [(i_2, (i_2 + 1) % count_2) for i_2 in range(count_2)]
+        back = [(b, a) for a, b in pairs]
+        lower, upper = ([], [])
+        for step in range(count_2 - 1):
+            if step % 2 == 0:
+                lower.append(lax.ppermute(lower[-1] if lower else shard, "exp", pairs))
+            else:
+                upper.append(lax.ppermute(upper[-1] if upper else shard, "exp", back))
+        parts = jnp.stack([*lower[::-1], shard, *upper])
+        shift = lax.axis_index("exp") - len(lower)
+        parts = parts[(jnp.arange(count_2) - shift) % count_2]
+        gathered = joined_along(parts, 0)
         laplacian = laplace_image(padded_2(sky_now, (("sky", 2),), 1))
         smooth = prior_weight * laplacian / denominator[:, None, None]
         sky_now = sky_now - (gathered.astype(jnp.float32) + smooth)

time: 340 us -> 418 us (1.23)
  the two profiles are of different devices: /device:TPU:2 before, /device:TPU:8 now
where the time goes in v1:
time: 418 us; the launch traced here: 416 us
  blocking collectives  152 us (36%)
  starting transfers between devices  133 us (32%)
  waiting for transfers between devices  61.9 us (15%)
  local copies, waits for them, and re-layouts  27.5 us (7%)
  matrix products  23.1 us (6%)
  other arithmetic  16.1 us (4%)
    ppermute x14, starting transfers between devices, per_device(): upper.append(lax.ppermute(upper[-1] if upper else shard, 'exp', back))  71.8 us
    all_to_all x1, blocking collectives, per_device(): lax.all_to_all(payload, 'exp', split_axis=0, concat_axis=0, tiled=True)  37.7 us
    unnamed x1, blocking collectives  35.3 us
    ppermute x16, starting transfers between devices, per_device(): lower.append(lax.ppermute(lower[-1] if lower else shard, 'exp', pairs))  33.4 us
    all_to_all x1, blocking collectives, per_device(): lax.all_to_all(sky_now[safe_rows].astype(jnp.bfloat16), 'sky', split_axis...  32.8 us
    all_to_all x1, blocking collectives, per_device(): lax.all_to_all(outgoing, 'sky', split_axis=0, concat_axis=0, tiled=True)  31.9 us
    all_to_all x1, waiting for transfers between devices, per_device(): lax.all_to_all(payload, 'exp', split_axis=0, concat_axis=0, tiled=True)  25 us
    all_to_all x1, waiting for transfers between devices, per_device(): lax.all_to_all(sky_now[safe_rows].astype(jnp.bfloat16), 'sky', split_axis...  21.6 us
  transfers between devices with their start and end apart: 37, of which 7 were waited for; matrix products, arithmetic and copies ran while one was open for 4% of the time, Pallas kernels for 0%

profile of v1, /device:TPU:8, one launch (start us, length us, event | category | flops | bytes accessed | tf_op | source)
XLA Modules:
  0.0 416.1 jit_solution(1886781331999272653)
XLA Ops:
  3.1 14.7 %all_to_all.36 = s32[32,2,1]{1,2,0:T(1,128)S(1)} all-to-all(s32[32,2,1]{1,2,0:T(1,128)S(1)} %bitcast.200), channel_id=1, replica_groups=mesh['exp'=16,'sky'=32] {'sky'}, dimensions={0} | all-to-all | bytes 512 | tf_op jit(solution)/shard_map/all_to_all | solution.py:100
  19.3 3.3 gather_fusion
  22.6 5.3 %all-to-all-start.1 = ((bf16[64,128,128]{2,1,0:T(8,128)(2,1)}), bf16[64,128,128]{2,1,0:T(8,128)(2,1)S(1)}, u32[]{:S(2)}, u32[]{:S(2)}) async-start(bf16[64,128,128]{2,1,0:T(8,128)(2,1)} %gather_fusion), calls=%async_computation.1 | async-start | bytes 4194304 | tf_op jit(solution)/shard_map/all_to_all | solution.py:111
  29.6 3.2 copy.148
  32.8 21.6 %all-to-all-done.1 = bf16[64,128,128]{2,1,0:T(8,128)(2,1)S(1)} async-done(((bf16[64,128,128]{2,1,0:T(8,128)(2,1)}), bf16[64,128,128]{2,1,0:T(8,128)(2,1)S(1)}, u32[]{:S(2)}, u32[]{:S(2)}) %all-to-all-start.1) | async-done | bytes 2097184 | tf_op jit(solution)/shard_map/all_to_all | solution.py:111
  55.1 5.0 %fusion.1 = bf16[32,2,128,128]{3,2,1,0:T(8,128)(2,1)S(1)} fusion(bf16[1,32,2,128,128]{4,3,2,1,0:T(8,128)(2,1)} %param.8, f32[32,2]{1,0:T(8,128)S(1)} %copy.104, bf16[32,2,2,128,128]{4,3,2,1,0:T(8,128)(2,1)} %bitcast.190, bf16[32,128,128]{2,1,0:T(8,128)(2,1)S(1)} %gather_fusion.1), kind=kOutput, calls=%fused_computation.12 | convolution fusion | flops 542113792 | bytes 9437440 | tf_op jit(solution)/shard_map/fetv,fewv->fetw/dot_general | solution.py:47
  60.2 3.6 bitcast_convert_fusion.1
  66.4 7.5 %all-to-all-start.2 = ((bf16[64,128,128]{2,1,0:T(8,128)(2,1)}), bf16[64,128,128]{2,1,0:T(8,128)(2,1)S(1)}, u32[]{:S(2)}, u32[]{:S(2)}) async-start(bf16[64,128,128]{2,1,0:T(8,128)(2,1)} %broadcast_select_fusion.1), calls=%async_computation.2 | async-start | bytes 4194304 | tf_op jit(solution)/shard_map/all_to_all | solution.py:121
  76.1 35.3 %all-reduce.2 = f32[256]{0:T(256)S(1)} all-reduce(f32[256]{0:T(256)S(1)} %multiply_dynamic-update-slice_fusion), channel_id=2, replica_groups=mesh['exp'=16,'sky'=32] {'exp'}, use_global_device_ids=true, to_apply=%add.2 | all-reduce | flops 256 | bytes 2048
  113.7 6.7 %all-to-all-start.3 = ((bf16[16,128,128]{2,1,0:T(8,128)(2,1)}), bf16[16,128,128]{2,1,0:T(8,128)(2,1)S(1)}, u32[]{:S(2)}, u32[]{:S(2)}) async-start(bf16[16,128,128]{2,1,0:T(8,128)(2,1)} %copy.108), calls=%async_computation.3 | async-start | bytes 1048576 | tf_op jit(solution)/shard_map/all_to_all | solution.py:134
  121.2 25.0 %all-to-all-done.3 = bf16[16,128,128]{2,1,0:T(8,128)(2,1)S(1)} async-done(((bf16[16,128,128]{2,1,0:T(8,128)(2,1)}), bf16[16,128,128]{2,1,0:T(8,128)(2,1)S(1)}, u32[]{:S(2)}, u32[]{:S(2)}) %all-to-all-start.3) | async-done | bytes 524320 | tf_op jit(solution)/shard_map/all_to_all | solution.py:134
  146.9 2.2 collective-permute-start
  149.2 4.8 %collective-permute-done = bf16[1,128,128]{2,1,0:T(8,128)(2,1)S(1)} collective-permute-done((bf16[1,128,128]{2,1,0:T(8,128)(2,1)S(1)}, bf16[1,128,128]{2,1,0:T(8,128)(2,1)S(1)}, u32[]{:S(2)}, u32[]{:S(2)}) %collective-permute-start) | collective-permute-done | bytes 32800 | tf_op jit(solution)/shard_map/ppermute | solution.py:147
  153.9 2.4 collective-permute-start.1
  156.3 4.7 %collective-permute-start.8 = (bf16[1,128,128]{2,1,0:T(8,128)(2,1)S(1)}, bf16[1,128,128]{2,1,0:T(8,128)(2,1)S(1)}, u32[]{:S(2)}, u32[]{:S(2)}) collective-permute-start(bf16[1,128,128]{2,1,0:T(8,128)(2,1)S(1)} %fusion.60), channel_id=1, source_target_pairs={{32,0},{64,32},{96,64},{128,96},{160,128},{192,160},{224,192},{256... | collective-permute-start | bytes 98312 | tf_op jit(solution)/shard_map/ppermute | solution.py:149
  161.0 1.9 collective-permute-start.2
  162.9 5.1 %collective-permute-start.9 = (bf16[1,128,128]{2,1,0:T(8,128)(2,1)S(1)}, bf16[1,128,128]{2,1,0:T(8,128)(2,1)S(1)}, u32[]{:S(2)}, u32[]{:S(2)}) collective-permute-start(bf16[1,128,128]{2,1,0:T(8,128)(2,1)S(1)} %collective-permute-done.8), channel_id=1, source_target_pairs={{32,0},{64,32},{96,64},{128,96},{160,128},{192,160},{224,192},{256... | collective-permute-start | bytes 98312 | tf_op jit(solution)/shard_map/ppermute | solution.py:149
  173.6 2.4 collective-permute-start.15
  176.0 5.1 %collective-permute-start.10 = (bf16[1,128,128]{2,1,0:T(8,128)(2,1)S(1)}, bf16[1,128,128]{2,1,0:T(8,128)(2,1)S(1)}, u32[]{:S(2)}, u32[]{:S(2)}) collective-permute-start(bf16[1,128,128]{2,1,0:T(8,128)(2,1)S(1)} %collective-permute-done.9), channel_id=1, source_target_pairs={{32,0},{64,32},{96,64},{128,96},{160,128},{192,160},{224,192},{256... | collective-permute-start | bytes 98312 | tf_op jit(solution)/shard_map/ppermute | solution.py:149
  181.2 1.9 collective-permute-start.4
  183.1 5.2 %collective-permute-start.11 = (bf16[1,128,128]{2,1,0:T(8,128)(2,1)S(1)}, bf16[1,128,128]{2,1,0:T(8,128)(2,1)S(1)}, u32[]{:S(2)}, u32[]{:S(2)}) collective-permute-start(bf16[1,128,128]{2,1,0:T(8,128)(2,1)S(1)} %collective-permute-done.10), channel_id=1, source_target_pairs={{32,0},{64,32},{96,64},{128,96},{160,128},{192,160},{224,192},{256... | collective-permute-start | bytes 98312 | tf_op jit(solution)/shard_map/ppermute | solution.py:149
  192.4 5.1 %collective-permute-start.12 = (bf16[1,128,128]{2,1,0:T(8,128)(2,1)S(1)}, bf16[1,128,128]{2,1,0:T(8,128)(2,1)S(1)}, u32[]{:S(2)}, u32[]{:S(2)}) collective-permute-start(bf16[1,128,128]{2,1,0:T(8,128)(2,1)S(1)} %collective-permute-done.11), channel_id=1, source_target_pairs={{32,0},{64,32},{96,64},{128,96},{160,128},{192,160},{224,192},{256... | collective-permute-start | bytes 98312 | tf_op jit(solution)/shard_map/ppermute | solution.py:149
  197.5 2.1 collective-permute-start.6
  200.8 5.1 %collective-permute-start.13 = (bf16[1,128,128]{2,1,0:T(8,128)(2,1)S(1)}, bf16[1,128,128]{2,1,0:T(8,128)(2,1)S(1)}, u32[]{:S(2)}, u32[]{:S(2)}) collective-permute-start(bf16[1,128,128]{2,1,0:T(8,128)(2,1)S(1)} %collective-permute-done.12), channel_id=1, source_target_pairs={{32,0},{64,32},{96,64},{128,96},{160,128},{192,160},{224,192},{256... | collective-permute-start | bytes 98312 | tf_op jit(solution)/shard_map/ppermute | solution.py:149
  208.4 5.1 %collective-permute-start.14 = (bf16[1,128,128]{2,1,0:T(8,128)(2,1)S(1)}, bf16[1,128,128]{2,1,0:T(8,128)(2,1)S(1)}, u32[]{:S(2)}, u32[]{:S(2)}) collective-permute-start(bf16[1,128,128]{2,1,0:T(8,128)(2,1)S(1)} %collective-permute-done.13), channel_id=1, source_target_pairs={{32,0},{64,32},{96,64},{128,96},{160,128},{192,160},{224,192},{256... | collective-permute-start | bytes 98312 | tf_op jit(solution)/shard_map/ppermute | solution.py:149
  218.0 2.2 gather_fusion.4
  220.2 32.8 %all_to_all.37 = bf16[64,128,128]{2,1,0:T(8,128)(2,1)} all-to-all(bf16[64,128,128]{2,1,0:T(8,128)(2,1)} %gather_fusion.4), channel_id=1, replica_groups=mesh['exp'=16,'sky'=32] {'sky'}, dimensions={0} | all-to-all | bytes 4194304 | tf_op jit(solution)/shard_map/all_to_all | solution.py:111
  253.0 2.5 gather_fusion.5
  255.5 6.4 %fusion.3 = bf16[32,2,128,128]{3,2,1,0:T(8,128)(2,1)} fusion(bf16[1,32,2,128,128]{4,3,2,1,0:T(8,128)(2,1)} %param.8, f32[32,2]{1,0:T(8,128)S(1)} %copy.104, bf16[32,2,2,128,128]{4,3,2,1,0:T(8,128)(2,1)} %bitcast.192, bf16[32,128,128]{2,1,0:T(8,128)(2,1)S(1)} %gather_fusion.5), kind=kOutput, calls=%fused_computation.14 | convolution fusion | flops 542113792 | bytes 9437440 | tf_op jit(solution)/shard_map/fetv,fewv->fetw/dot_general | solution.py:47
  261.9 4.3 %bitcast_convert_fusion = bf16[32,128,128]{2,1,0:T(8,128)(2,1)S(1)} fusion(bf16[32,2,128,128]{3,2,1,0:T(8,128)(2,1)} %fusion.3, bf16[32,2,2,128,128]{4,3,2,1,0:T(8,128)(2,1)} %bitcast.193), kind=kOutput, calls=%fused_computation.20 | convolution fusion | flops 538443776 | bytes 7340032 | tf_op jit(solution)/shard_map/fetw,fewv->fetv/dot_general | solution.py:58
  266.2 2.3 gather_fusion.6
  270.2 31.9 %all_to_all.38 = bf16[64,128,128]{2,1,0:T(8,128)(2,1)S(1)} all-to-all(bf16[64,128,128]{2,1,0:T(8,128)(2,1)S(1)} %broadcast_select_fusion), channel_id=1, replica_groups=mesh['exp'=16,'sky'=32] {'sky'}, dimensions={0} | all-to-all | bytes 4194304 | tf_op jit(solution)/shard_map/all_to_all | solution.py:121
  303.6 37.7 %all_to_all.39 = bf16[16,128,128]{2,1,0:T(8,128)(2,1)S(1)} all-to-all(bf16[16,128,128]{2,1,0:T(8,128)(2,1)S(1)} %copy.131), channel_id=1, replica_groups=mesh['exp'=16,'sky'=32] {'exp'}, dimensions={0} | all-to-all | bytes 1048576 | tf_op jit(solution)/shard_map/all_to_all | solution.py:134
  342.0 3.7 collective-permute-start.17
  345.7 4.9 %collective-permute-done.17 = bf16[1,128,128]{2,1,0:T(8,128)(2,1)S(1)} collective-permute-done((bf16[1,128,128]{2,1,0:T(8,128)(2,1)S(1)}, bf16[1,128,128]{2,1,0:T(8,128)(2,1)S(1)}, u32[]{:S(2)}, u32[]{:S(2)}) %collective-permute-start.17) | collective-permute-done | bytes 32800 | tf_op jit(solution)/shard_map/ppermute | solution.py:147
  352.5 5.1 %collective-permute-start.25 = (bf16[1,128,128]{2,1,0:T(8,128)(2,1)S(1)}, bf16[1,128,128]{2,1,0:T(8,128)(2,1)S(1)}, u32[]{:S(2)}, u32[]{:S(2)}) collective-permute-start(bf16[1,128,128]{2,1,0:T(8,128)(2,1)S(1)} %fusion.61), channel_id=1, source_target_pairs={{32,0},{64,32},{96,64},{128,96},{160,128},{192,160},{224,192},{256... | collective-permute-start | bytes 98312 | tf_op jit(solution)/shard_map/ppermute | solution.py:149
  357.6 1.9 collective-permute-start.19
  359.5 5.1 %collective-permute-start.26 = (bf16[1,128,128]{2,1,0:T(8,128)(2,1)S(1)}, bf16[1,128,128]{2,1,0:T(8,128)(2,1)S(1)}, u32[]{:S(2)}, u32[]{:S(2)}) collective-permute-start(bf16[1,128,128]{2,1,0:T(8,128)(2,1)S(1)} %collective-permute-done.25), channel_id=1, source_target_pairs={{32,0},{64,32},{96,64},{128,96},{160,128},{192,160},{224,192},{256... | collective-permute-start | bytes 98312 | tf_op jit(solution)/shard_map/ppermute | solution.py:149
  366.6 5.4 %collective-permute-start.27 = (bf16[1,128,128]{2,1,0:T(8,128)(2,1)S(1)}, bf16[1,128,128]{2,1,0:T(8,128)(2,1)S(1)}, u32[]{:S(2)}, u32[]{:S(2)}) collective-permute-start(bf16[1,128,128]{2,1,0:T(8,128)(2,1)S(1)} %collective-permute-done.26), channel_id=1, source_target_pairs={{32,0},{64,32},{96,64},{128,96},{160,128},{192,160},{224,192},{256... | collective-permute-start | bytes 98312 | tf_op jit(solution)/shard_map/ppermute | solution.py:149
  372.0 1.9 collective-permute-start.21
  374.0 5.1 %collective-permute-start.28 = (bf16[1,128,128]{2,1,0:T(8,128)(2,1)S(1)}, bf16[1,128,128]{2,1,0:T(8,128)(2,1)S(1)}, u32[]{:S(2)}, u32[]{:S(2)}) collective-permute-start(bf16[1,128,128]{2,1,0:T(8,128)(2,1)S(1)} %collective-permute-done.27), channel_id=1, source_target_pairs={{32,0},{64,32},{96,64},{128,96},{160,128},{192,160},{224,192},{256... | collective-permute-start | bytes 98312 | tf_op jit(solution)/shard_map/ppermute | solution.py:149
  379.1 1.9 collective-permute-start.22
  381.7 1.9 collective-permute-start.33
  384.0 2.4 collective-permute-start.32
  386.8 4.3 %collective-permute-done.32 = f32[16,128,1]{1,0,2:T(8,128)S(1)} collective-permute-done((f32[16,128,1]{1,0,2:T(8,128)S(1)}, f32[16,128,1]{1,0,2:T(8,128)S(1)}, u32[]{:S(2)}, u32[]{:S(2)}) %collective-permute-start.32) | collective-permute-done | bytes 8224 | tf_op jit(solution)/shard_map/ppermute | solution.py:24
  391.5 5.1 %collective-permute-start.29 = (bf16[1,128,128]{2,1,0:T(8,128)(2,1)S(1)}, bf16[1,128,128]{2,1,0:T(8,128)(2,1)S(1)}, u32[]{:S(2)}, u32[]{:S(2)}) collective-permute-start(bf16[1,128,128]{2,1,0:T(8,128)(2,1)S(1)} %collective-permute-done.28), channel_id=1, source_target_pairs={{32,0},{64,32},{96,64},{128,96},{160,128},{192,160},{224,192},{256... | collective-permute-start | bytes 98312 | tf_op jit(solution)/shard_map/ppermute | solution.py:149
  399.8 5.1 %collective-permute-start.30 = (bf16[1,128,128]{2,1,0:T(8,128)(2,1)S(1)}, bf16[1,128,128]{2,1,0:T(8,128)(2,1)S(1)}, u32[]{:S(2)}, u32[]{:S(2)}) collective-permute-start(bf16[1,128,128]{2,1,0:T(8,128)(2,1)S(1)} %collective-permute-done.29), channel_id=1, source_target_pairs={{32,0},{64,32},{96,64},{128,96},{160,128},{192,160},{224,192},{256... | collective-permute-start | bytes 98312 | tf_op jit(solution)/shard_map/ppermute | solution.py:149
  407.4 5.1 %collective-permute-start.31 = (bf16[1,128,128]{2,1,0:T(8,128)(2,1)S(1)}, bf16[1,128,128]{2,1,0:T(8,128)(2,1)S(1)}, u32[]{:S(2)}, u32[]{:S(2)}) collective-permute-start(bf16[1,128,128]{2,1,0:T(8,128)(2,1)S(1)} %collective-permute-done.30), channel_id=1, source_target_pairs={{32,0},{64,32},{96,64},{128,96},{160,128},{192,160},{224,192},{256... | collective-permute-start | bytes 98312 | tf_op jit(solution)/shard_map/ppermute | solution.py:149
  (165 shorter events, 50.8 us)
Async XLA Ops:
  22.6 5.3 %copy-start.13 = (bf16[1,32,2]{1,2,0:T(2,128)(2,1)S(1)}, bf16[1,32,2]{1,2,0:T(2,128)(2,1)}, u32[]{:S(2)}) copy-start(bf16[1,32,2]{1,2,0:T(2,128)(2,1)} %param.9) | copy-start | bytes 388
  22.6 5.4 %copy-start.10 = (s32[1,32,2,2]{1,3,2,0:T(2,128)S(1)}, s32[1,32,2,2]{1,3,2,0:T(2,128)}, u32[]{:S(2)}) copy-start(s32[1,32,2,2]{1,3,2,0:T(2,128)} %param.12) | copy-start | bytes 1540
  22.6 5.6 %copy-start.1 = (bf16[8,128,128]{2,1,0:T(8,128)(2,1)S(1)}, bf16[8,128,128]{2,1,0:T(8,128)(2,1)}, u32[]{:S(2)}) copy-start(bf16[8,128,128]{2,1,0:T(8,128)(2,1)} %param.13) | copy-start | bytes 786436
  22.6 31.8 %all-to-all-start.1 = ((bf16[64,128,128]{2,1,0:T(8,128)(2,1)}), bf16[64,128,128]{2,1,0:T(8,128)(2,1)S(1)}, u32[]{:S(2)}, u32[]{:S(2)}) async-start(bf16[64,128,128]{2,1,0:T(8,128)(2,1)} %gather_fusion), calls=%async_computation.1 | async-start | bytes 4194304 | tf_op jit(solution)/shard_map/all_to_all | solution.py:111
  32.8 27.4 %copy-start.4 = (s32[1024]{0:T(1024)}, s32[1024]{0:T(1024)S(1)}, u32[]{:S(2)}) copy-start(s32[1024]{0:T(1024)S(1)} %pad_clamp_fusion.2) | copy-start | bytes 12292
  32.8 31.0 %copy-start.3 = (s32[1024]{0:T(1024)}, s32[1024]{0:T(1024)S(1)}, u32[]{:S(2)}) copy-start(s32[1024]{0:T(1024)S(1)} %pad_clamp_fusion.1) | copy-start | bytes 12292
  32.8 32.0 %copy-start.8 = (pred[64]{0:T(512)(128)(4,1)}, pred[64]{0:T(512)(128)(4,1)S(1)}, u32[]{:S(2)}) copy-start(pred[64]{0:T(512)(128)(4,1)S(1)} %fusion.55) | copy-start | bytes 196
  66.4 45.0 %all-to-all-start.2 = ((bf16[64,128,128]{2,1,0:T(8,128)(2,1)}), bf16[64,128,128]{2,1,0:T(8,128)(2,1)S(1)}, u32[]{:S(2)}, u32[]{:S(2)}) async-start(bf16[64,128,128]{2,1,0:T(8,128)(2,1)} %broadcast_select_fusion.1), calls=%async_computation.2 | async-start | bytes 4194304 | tf_op jit(solution)/shard_map/all_to_all | solution.py:121
  75.9 37.8 %copy-start.6 = (s32[64]{0:T(128)}, s32[64]{0:T(128)S(1)}, u32[]{:S(2)}) copy-start(s32[64]{0:T(128)S(1)} %eq.67) | copy-start | bytes 772
  112.8 57.3 %copy-start = (f32[16,128,128]{2,1,0:T(8,128)S(1)}, f32[16,128,128]{2,1,0:T(8,128)}, u32[]{:S(2)}) copy-start(f32[16,128,128]{2,1,0:T(8,128)} %param.7) | copy-start | bytes 3145732
  113.7 32.5 %all-to-all-start.3 = ((bf16[16,128,128]{2,1,0:T(8,128)(2,1)}), bf16[16,128,128]{2,1,0:T(8,128)(2,1)S(1)}, u32[]{:S(2)}, u32[]{:S(2)}) async-start(bf16[16,128,128]{2,1,0:T(8,128)(2,1)} %copy.108), calls=%async_computation.3 | async-start | bytes 1048576 | tf_op jit(solution)/shard_map/all_to_all | solution.py:134
  120.6 47.5 %copy-start.11 = (f32[16]{0:T(128)}, f32[16]{0:T(128)S(1)}, u32[]{:S(2)}) copy-start(f32[16]{0:T(128)S(1)} %multiply_add_fusion) | copy-start | bytes 196
  146.9 7.0 %collective-permute-start = (bf16[1,128,128]{2,1,0:T(8,128)(2,1)S(1)}, bf16[1,128,128]{2,1,0:T(8,128)(2,1)S(1)}, u32[]{:S(2)}, u32[]{:S(2)}) collective-permute-start(bf16[1,128,128]{2,1,0:T(8,128)(2,1)S(1)} %fusion.60), channel_id=1, source_target_pairs={{0,32},{32,64},{64,96},{96,128},{128,160},{160,192},{192,224},{224... | collective-permute-start | bytes 98312 | tf_op jit(solution)/shard_map/ppermute | solution.py:147
  153.9 7.1 %collective-permute-start.1 = (bf16[1,128,128]{2,1,0:T(8,128)(2,1)S(1)}, bf16[1,128,128]{2,1,0:T(8,128)(2,1)S(1)}, u32[]{:S(2)}, u32[]{:S(2)}) collective-permute-start(bf16[1,128,128]{2,1,0:T(8,128)(2,1)S(1)} %collective-permute-done), channel_id=1, source_target_pairs={{0,32},{32,64},{64,96},{96,128},{128,160},{160,192},{192,224},{224... | collective-permute-start | bytes 98312 | tf_op jit(solution)/shard_map/ppermute | solution.py:147
  156.3 6.6 %collective-permute-start.8 = (bf16[1,128,128]{2,1,0:T(8,128)(2,1)S(1)}, bf16[1,128,128]{2,1,0:T(8,128)(2,1)S(1)}, u32[]{:S(2)}, u32[]{:S(2)}) collective-permute-start(bf16[1,128,128]{2,1,0:T(8,128)(2,1)S(1)} %fusion.60), channel_id=1, source_target_pairs={{32,0},{64,32},{96,64},{128,96},{160,128},{192,160},{224,192},{256... | collective-permute-start | bytes 98312 | tf_op jit(solution)/shard_map/ppermute | solution.py:149
  161.0 7.1 %collective-permute-start.2 = (bf16[1,128,128]{2,1,0:T(8,128)(2,1)S(1)}, bf16[1,128,128]{2,1,0:T(8,128)(2,1)S(1)}, u32[]{:S(2)}, u32[]{:S(2)}) collective-permute-start(bf16[1,128,128]{2,1,0:T(8,128)(2,1)S(1)} %collective-permute-done.1), channel_id=1, source_target_pairs={{0,32},{32,64},{64,96},{96,128},{128,160},{160,192},{192,224},{224... | collective-permute-start | bytes 98312 | tf_op jit(solution)/shard_map/ppermute | solution.py:147
  162.9 13.1 %collective-permute-start.9 = (bf16[1,128,128]{2,1,0:T(8,128)(2,1)S(1)}, bf16[1,128,128]{2,1,0:T(8,128)(2,1)S(1)}, u32[]{:S(2)}, u32[]{:S(2)}) collective-permute-start(bf16[1,128,128]{2,1,0:T(8,128)(2,1)S(1)} %collective-permute-done.8), channel_id=1, source_target_pairs={{32,0},{64,32},{96,64},{128,96},{160,128},{192,160},{224,192},{256... | collective-permute-start | bytes 98312 | tf_op jit(solution)/shard_map/ppermute | solution.py:149
  168.1 13.0 %collective-permute-start.3 = (bf16[1,128,128]{2,1,0:T(8,128)(2,1)S(1)}, bf16[1,128,128]{2,1,0:T(8,128)(2,1)S(1)}, u32[]{:S(2)}, u32[]{:S(2)}) collective-permute-start(bf16[1,128,128]{2,1,0:T(8,128)(2,1)S(1)} %collective-permute-done.2), channel_id=1, source_target_pairs={{0,32},{32,64},{64,96},{96,128},{128,160},{160,192},{192,224},{224... | collective-permute-start | bytes 98312 | tf_op jit(solution)/shard_map/ppermute | solution.py:147
  171.3 19.6 %collective-permute-start.16 = (f32[16,128,1]{1,0,2:T(8,128)}, f32[16,128,1]{1,0,2:T(8,128)S(1)}, u32[]{:S(2)}, u32[]{:S(2)}) collective-permute-start(f32[16,128,1]{1,0,2:T(8,128)} %copy.146), channel_id=1, source_target_pairs={{1,0},{2,1},{3,2},{4,3},{5,4},{6,5},{7,6},{8,7},{9,8},{10,9},{11,1... | collective-permute-start | bytes 24584 | tf_op jit(solution)/shard_map/ppermute | solution.py:26
  173.6 17.7 %collective-permute-start.15 = (f32[16,128,1]{1,0,2:T(8,128)S(1)}, f32[16,128,1]{1,0,2:T(8,128)}, u32[]{:S(2)}, u32[]{:S(2)}) collective-permute-start(f32[16,128,1]{1,0,2:T(8,128)S(1)} %copy.145), channel_id=1, source_target_pairs={{0,1},{1,2},{2,3},{3,4},{4,5},{5,6},{6,7},{7,8},{8,9},{9,10},{10,1... | collective-permute-start | bytes 24584 | tf_op jit(solution)/shard_map/ppermute | solution.py:24
  176.0 7.1 %collective-permute-start.10 = (bf16[1,128,128]{2,1,0:T(8,128)(2,1)S(1)}, bf16[1,128,128]{2,1,0:T(8,128)(2,1)S(1)}, u32[]{:S(2)}, u32[]{:S(2)}) collective-permute-start(bf16[1,128,128]{2,1,0:T(8,128)(2,1)S(1)} %collective-permute-done.9), channel_id=1, source_target_pairs={{32,0},{64,32},{96,64},{128,96},{160,128},{192,160},{224,192},{256... | collective-permute-start | bytes 98312 | tf_op jit(solution)/shard_map/ppermute | solution.py:149
  181.2 7.2 %collective-permute-start.4 = (bf16[1,128,128]{2,1,0:T(8,128)(2,1)S(1)}, bf16[1,128,128]{2,1,0:T(8,128)(2,1)S(1)}, u32[]{:S(2)}, u32[]{:S(2)}) collective-permute-start(bf16[1,128,128]{2,1,0:T(8,128)(2,1)S(1)} %collective-permute-done.3), channel_id=1, source_target_pairs={{0,32},{32,64},{64,96},{96,128},{128,160},{160,192},{192,224},{224... | collective-permute-start | bytes 98312 | tf_op jit(solution)/shard_map/ppermute | solution.py:147
  183.1 9.2 %collective-permute-start.11 = (bf16[1,128,128]{2,1,0:T(8,128)(2,1)S(1)}, bf16[1,128,128]{2,1,0:T(8,128)(2,1)S(1)}, u32[]{:S(2)}, u32[]{:S(2)}) collective-permute-start(bf16[1,128,128]{2,1,0:T(8,128)(2,1)S(1)} %collective-permute-done.10), channel_id=1, source_target_pairs={{32,0},{64,32},{96,64},{128,96},{160,128},{192,160},{224,192},{256... | collective-permute-start | bytes 98312 | tf_op jit(solution)/shard_map/ppermute | solution.py:149
  188.4 9.1 %collective-permute-start.5 = (bf16[1,128,128]{2,1,0:T(8,128)(2,1)S(1)}, bf16[1,128,128]{2,1,0:T(8,128)(2,1)S(1)}, u32[]{:S(2)}, u32[]{:S(2)}) collective-permute-start(bf16[1,128,128]{2,1,0:T(8,128)(2,1)S(1)} %collective-permute-done.4), channel_id=1, source_target_pairs={{0,32},{32,64},{64,96},{96,128},{128,160},{160,192},{192,224},{224... | collective-permute-start | bytes 98312 | tf_op jit(solution)/shard_map/ppermute | solution.py:147
  192.4 8.5 %collective-permute-start.12 = (bf16[1,128,128]{2,1,0:T(8,128)(2,1)S(1)}, bf16[1,128,128]{2,1,0:T(8,128)(2,1)S(1)}, u32[]{:S(2)}, u32[]{:S(2)}) collective-permute-start(bf16[1,128,128]{2,1,0:T(8,128)(2,1)S(1)} %collective-permute-done.11), channel_id=1, source_target_pairs={{32,0},{64,32},{96,64},{128,96},{160,128},{192,160},{224,192},{256... | collective-permute-start | bytes 98312 | tf_op jit(solution)/shard_map/ppermute | solution.py:149
  197.5 8.5 %collective-permute-start.6 = (bf16[1,128,128]{2,1,0:T(8,128)(2,1)S(1)}, bf16[1,128,128]{2,1,0:T(8,128)(2,1)S(1)}, u32[]{:S(2)}, u32[]{:S(2)}) collective-permute-start(bf16[1,128,128]{2,1,0:T(8,128)(2,1)S(1)} %collective-permute-done.5), channel_id=1, source_target_pairs={{0,32},{32,64},{64,96},{96,128},{128,160},{160,192},{192,224},{224... | collective-permute-start | bytes 98312 | tf_op jit(solution)/shard_map/ppermute | solution.py:147
  200.8 7.6 %collective-permute-start.13 = (bf16[1,128,128]{2,1,0:T(8,128)(2,1)S(1)}, bf16[1,128,128]{2,1,0:T(8,128)(2,1)S(1)}, u32[]{:S(2)}, u32[]{:S(2)}) collective-permute-start(bf16[1,128,128]{2,1,0:T(8,128)(2,1)S(1)} %collective-permute-done.12), channel_id=1, source_target_pairs={{32,0},{64,32},{96,64},{128,96},{160,128},{192,160},{224,192},{256... | collective-permute-start | bytes 98312 | tf_op jit(solution)/shard_map/ppermute | solution.py:149
  206.0 7.6 %collective-permute-start.7 = (bf16[1,128,128]{2,1,0:T(8,128)(2,1)S(1)}, bf16[1,128,128]{2,1,0:T(8,128)(2,1)S(1)}, u32[]{:S(2)}, u32[]{:S(2)}) collective-permute-start(bf16[1,128,128]{2,1,0:T(8,128)(2,1)S(1)} %collective-permute-done.6), channel_id=1, source_target_pairs={{0,32},{32,64},{64,96},{96,128},{128,160},{160,192},{192,224},{224... | collective-permute-start | bytes 98312 | tf_op jit(solution)/shard_map/ppermute | solution.py:147
  208.4 6.7 %collective-permute-start.14 = (bf16[1,128,128]{2,1,0:T(8,128)(2,1)S(1)}, bf16[1,128,128]{2,1,0:T(8,128)(2,1)S(1)}, u32[]{:S(2)}, u32[]{:S(2)}) collective-permute-start(bf16[1,128,128]{2,1,0:T(8,128)(2,1)S(1)} %collective-permute-done.13), channel_id=1, source_target_pairs={{32,0},{64,32},{96,64},{128,96},{160,128},{192,160},{224,192},{256... | collective-permute-start | bytes 98312 | tf_op jit(solution)/shard_map/ppermute | solution.py:149
  270.2 31.9 %copy-start.7 = (s32[64]{0:T(128)S(1)}, s32[64]{0:T(128)}, u32[]{:S(2)}) copy-start(s32[64]{0:T(128)} %copy-done.6) | copy-start | bytes 772
  342.0 8.5 %collective-permute-start.17 = (bf16[1,128,128]{2,1,0:T(8,128)(2,1)S(1)}, bf16[1,128,128]{2,1,0:T(8,128)(2,1)S(1)}, u32[]{:S(2)}, u32[]{:S(2)}) collective-permute-start(bf16[1,128,128]{2,1,0:T(8,128)(2,1)S(1)} %fusion.61), channel_id=1, source_target_pairs={{0,32},{32,64},{64,96},{96,128},{128,160},{160,192},{192,224},{224... | collective-permute-start | bytes 98312 | tf_op jit(solution)/shard_map/ppermute | solution.py:147
  350.5 7.1 %collective-permute-start.18 = (bf16[1,128,128]{2,1,0:T(8,128)(2,1)S(1)}, bf16[1,128,128]{2,1,0:T(8,128)(2,1)S(1)}, u32[]{:S(2)}, u32[]{:S(2)}) collective-permute-start(bf16[1,128,128]{2,1,0:T(8,128)(2,1)S(1)} %collective-permute-done.17), channel_id=1, source_target_pairs={{0,32},{32,64},{64,96},{96,128},{128,160},{160,192},{192,224},{224... | collective-permute-start | bytes 98312 | tf_op jit(solution)/shard_map/ppermute | solution.py:147
  352.5 7.1 %collective-permute-start.25 = (bf16[1,128,128]{2,1,0:T(8,128)(2,1)S(1)}, bf16[1,128,128]{2,1,0:T(8,128)(2,1)S(1)}, u32[]{:S(2)}, u32[]{:S(2)}) collective-permute-start(bf16[1,128,128]{2,1,0:T(8,128)(2,1)S(1)} %fusion.61), channel_id=1, source_target_pairs={{32,0},{64,32},{96,64},{128,96},{160,128},{192,160},{224,192},{256... | collective-permute-start | bytes 98312 | tf_op jit(solution)/shard_map/ppermute | solution.py:149
  357.6 7.1 %collective-permute-start.19 = (bf16[1,128,128]{2,1,0:T(8,128)(2,1)S(1)}, bf16[1,128,128]{2,1,0:T(8,128)(2,1)S(1)}, u32[]{:S(2)}, u32[]{:S(2)}) collective-permute-start(bf16[1,128,128]{2,1,0:T(8,128)(2,1)S(1)} %collective-permute-done.18), channel_id=1, source_target_pairs={{0,32},{32,64},{64,96},{96,128},{128,160},{160,192},{192,224},{224... | collective-permute-start | bytes 98312 | tf_op jit(solution)/shard_map/ppermute | solution.py:147
  359.5 7.1 %collective-permute-start.26 = (bf16[1,128,128]{2,1,0:T(8,128)(2,1)S(1)}, bf16[1,128,128]{2,1,0:T(8,128)(2,1)S(1)}, u32[]{:S(2)}, u32[]{:S(2)}) collective-permute-start(bf16[1,128,128]{2,1,0:T(8,128)(2,1)S(1)} %collective-permute-done.25), channel_id=1, source_target_pairs={{32,0},{64,32},{96,64},{128,96},{160,128},{192,160},{224,192},{256... | collective-permute-start | bytes 98312 | tf_op jit(solution)/shard_map/ppermute | solution.py:149
  364.7 7.3 %collective-permute-start.20 = (bf16[1,128,128]{2,1,0:T(8,128)(2,1)S(1)}, bf16[1,128,128]{2,1,0:T(8,128)(2,1)S(1)}, u32[]{:S(2)}, u32[]{:S(2)}) collective-permute-start(bf16[1,128,128]{2,1,0:T(8,128)(2,1)S(1)} %collective-permute-done.19), channel_id=1, source_target_pairs={{0,32},{32,64},{64,96},{96,128},{128,160},{160,192},{192,224},{224... | collective-permute-start | bytes 98312 | tf_op jit(solution)/shard_map/ppermute | solution.py:147
  366.6 7.3 %collective-permute-start.27 = (bf16[1,128,128]{2,1,0:T(8,128)(2,1)S(1)}, bf16[1,128,128]{2,1,0:T(8,128)(2,1)S(1)}, u32[]{:S(2)}, u32[]{:S(2)}) collective-permute-start(bf16[1,128,128]{2,1,0:T(8,128)(2,1)S(1)} %collective-permute-done.26), channel_id=1, source_target_pairs={{32,0},{64,32},{96,64},{128,96},{160,128},{192,160},{224,192},{256... | collective-permute-start | bytes 98312 | tf_op jit(solution)/shard_map/ppermute | solution.py:149
  372.0 7.1 %collective-permute-start.21 = (bf16[1,128,128]{2,1,0:T(8,128)(2,1)S(1)}, bf16[1,128,128]{2,1,0:T(8,128)(2,1)S(1)}, u32[]{:S(2)}, u32[]{:S(2)}) collective-permute-start(bf16[1,128,128]{2,1,0:T(8,128)(2,1)S(1)} %collective-permute-done.20), channel_id=1, source_target_pairs={{0,32},{32,64},{64,96},{96,128},{128,160},{160,192},{192,224},{224... | collective-permute-start | bytes 98312 | tf_op jit(solution)/shard_map/ppermute | solution.py:147
  374.0 17.5 %collective-permute-start.28 = (bf16[1,128,128]{2,1,0:T(8,128)(2,1)S(1)}, bf16[1,128,128]{2,1,0:T(8,128)(2,1)S(1)}, u32[]{:S(2)}, u32[]{:S(2)}) collective-permute-start(bf16[1,128,128]{2,1,0:T(8,128)(2,1)S(1)} %collective-permute-done.27), channel_id=1, source_target_pairs={{32,0},{64,32},{96,64},{128,96},{160,128},{192,160},{224,192},{256... | collective-permute-start | bytes 98312 | tf_op jit(solution)/shard_map/ppermute | solution.py:149
  379.1 17.5 %collective-permute-start.22 = (bf16[1,128,128]{2,1,0:T(8,128)(2,1)S(1)}, bf16[1,128,128]{2,1,0:T(8,128)(2,1)S(1)}, u32[]{:S(2)}, u32[]{:S(2)}) collective-permute-start(bf16[1,128,128]{2,1,0:T(8,128)(2,1)S(1)} %collective-permute-done.21), channel_id=1, source_target_pairs={{0,32},{32,64},{64,96},{96,128},{128,160},{160,192},{192,224},{224... | collective-permute-start | bytes 98312 | tf_op jit(solution)/shard_map/ppermute | solution.py:147
  381.7 4.7 %collective-permute-start.33 = (f32[16,128,1]{1,0,2:T(8,128)S(1)}, f32[16,128,1]{1,0,2:T(8,128)S(1)}, u32[]{:S(2)}, u32[]{:S(2)}) collective-permute-start(f32[16,128,1]{1,0,2:T(8,128)S(1)} %copy.133), channel_id=1, source_target_pairs={{1,0},{2,1},{3,2},{4,3},{5,4},{6,5},{7,6},{8,7},{9,8},{10,9},{11,1... | collective-permute-start | bytes 24584 | tf_op jit(solution)/shard_map/ppermute | solution.py:26
  384.0 7.1 %collective-permute-start.32 = (f32[16,128,1]{1,0,2:T(8,128)S(1)}, f32[16,128,1]{1,0,2:T(8,128)S(1)}, u32[]{:S(2)}, u32[]{:S(2)}) collective-permute-start(f32[16,128,1]{1,0,2:T(8,128)S(1)} %copy.132), channel_id=1, source_target_pairs={{0,1},{1,2},{2,3},{3,4},{4,5},{5,6},{6,7},{7,8},{8,9},{9,10},{10,1... | collective-permute-start | bytes 24584 | tf_op jit(solution)/shard_map/ppermute | solution.py:24
  391.5 8.3 %collective-permute-start.29 = (bf16[1,128,128]{2,1,0:T(8,128)(2,1)S(1)}, bf16[1,128,128]{2,1,0:T(8,128)(2,1)S(1)}, u32[]{:S(2)}, u32[]{:S(2)}) collective-permute-start(bf16[1,128,128]{2,1,0:T(8,128)(2,1)S(1)} %collective-permute-done.28), channel_id=1, source_target_pairs={{32,0},{64,32},{96,64},{128,96},{160,128},{192,160},{224,192},{256... | collective-permute-start | bytes 98312 | tf_op jit(solution)/shard_map/ppermute | solution.py:149
  396.6 8.3 %collective-permute-start.23 = (bf16[1,128,128]{2,1,0:T(8,128)(2,1)S(1)}, bf16[1,128,128]{2,1,0:T(8,128)(2,1)S(1)}, u32[]{:S(2)}, u32[]{:S(2)}) collective-permute-start(bf16[1,128,128]{2,1,0:T(8,128)(2,1)S(1)} %collective-permute-done.22), channel_id=1, source_target_pairs={{0,32},{32,64},{64,96},{96,128},{128,160},{160,192},{192,224},{224... | collective-permute-start | bytes 98312 | tf_op jit(solution)/shard_map/ppermute | solution.py:147
  399.8 7.6 %collective-permute-start.30 = (bf16[1,128,128]{2,1,0:T(8,128)(2,1)S(1)}, bf16[1,128,128]{2,1,0:T(8,128)(2,1)S(1)}, u32[]{:S(2)}, u32[]{:S(2)}) collective-permute-start(bf16[1,128,128]{2,1,0:T(8,128)(2,1)S(1)} %collective-permute-done.29), channel_id=1, source_target_pairs={{32,0},{64,32},{96,64},{128,96},{160,128},{192,160},{224,192},{256... | collective-permute-start | bytes 98312 | tf_op jit(solution)/shard_map/ppermute | solution.py:149
  404.9 7.6 %collective-permute-start.24 = (bf16[1,128,128]{2,1,0:T(8,128)(2,1)S(1)}, bf16[1,128,128]{2,1,0:T(8,128)(2,1)S(1)}, u32[]{:S(2)}, u32[]{:S(2)}) collective-permute-start(bf16[1,128,128]{2,1,0:T(8,128)(2,1)S(1)} %collective-permute-done.23), channel_id=1, source_target_pairs={{0,32},{32,64},{64,96},{96,128},{128,160},{160,192},{192,224},{224... | collective-permute-start | bytes 98312 | tf_op jit(solution)/shard_map/ppermute | solution.py:147
  407.4 7.5 %copy-start.12 = (f32[16]{0:T(128)S(1)}, f32[16]{0:T(128)}, u32[]{:S(2)}) copy-start(f32[16]{0:T(128)} %copy-done.11) | copy-start | bytes 196
  407.4 6.7 %collective-permute-start.31 = (bf16[1,128,128]{2,1,0:T(8,128)(2,1)S(1)}, bf16[1,128,128]{2,1,0:T(8,128)(2,1)S(1)}, u32[]{:S(2)}, u32[]{:S(2)}) collective-permute-start(bf16[1,128,128]{2,1,0:T(8,128)(2,1)S(1)} %collective-permute-done.30), channel_id=1, source_target_pairs={{32,0},{64,32},{96,64},{128,96},{160,128},{192,160},{224,192},{256... | collective-permute-start | bytes 98312 | tf_op jit(solution)/shard_map/ppermute | solution.py:149
  (3 other events, 8.8 us)
